TPU v7x, 256 devices: a whole 4x4x8 slice. The times are simulated.
256 devices in a mesh: dp: 16 (over y_lo, z), fsdp: 16 (over x, y_hi, core).
Axes of the slice: x: 4, y: 4 (y_hi: 2, y_lo: 2; y = y_hi * 2 + y_lo), z: 8, core: 2. Of those that a mesh axis runs over, the one named last changes fastest.
Arguments:
- latents: bfloat16 [1024, 8, 8, 640], P(('dp', 'fsdp'))
- bucket: int32 [1024], P(('dp', 'fsdp')), may hold values from 0 to 39
- cotangent: bfloat16 [1024, 4, 4, 640], P(('dp', 'fsdp')), may hold values from -6 to 6
- tile_count: int32 [256], P(('dp', 'fsdp')), may hold values from 1 to 4, as said below
- cond_table: float32 [40, 640], replicated, may hold values from -3 to 3
- norm_gain: float32 [640], replicated, may hold values from 0.1 to 1.9
- norm_shift: float32 [640], replicated, may hold values from -3 to 3
- conv_bias: float32 [640], replicated, may hold values from -3 to 3
- down_bias: float32 [640], replicated, may hold values from -3 to 3
- conv_weight: bfloat16 [5760, 640], P('fsdp'), may hold values from -0.078125 to 0.078125
- down_weight: bfloat16 [5760, 640], P('fsdp'), may hold values from -0.078125 to 0.078125
Outputs:
- block_output: bfloat16 [1024, 4, 4, 640], P(('dp', 'fsdp'))
- grad_input: bfloat16 [1024, 8, 8, 640], P(('dp', 'fsdp'))
- grad_conv: float32 [5760, 640], P('fsdp')
- grad_affine: float32 [3, 640], replicated
Inputs may be any that keep to these rules, and one draw needn't show every extreme that they name: Slots 0 to tile_count - 1 of a device are live; some device holds exactly 4 live tiles.
All inputs are finite; a program needn't handle non-finite values.
Results may differ from a plain program's by a relative error of at most 0.005.
Values may be sent and summed in bfloat16 or wider, within the bound.
No kernel may reach another device: no remote copies, remote signals or barrier semaphores. Data moves between devices by JAX's collectives and lax.ppermute only.
A program may use at most 128 MiB of HBM per device.

v0:
```python
import math

import jax
import jax.numpy as jnp
from jax import lax
from jax.sharding import PartitionSpec as P

GROUPS = 32
CONV_DIMS = ("NHWC", "HWIO", "NHWC")
BACK_DIMS = ("NHWC", "HWOI", "NHWC")


def group_mean(channel_sums, per_group):
    tiles, channels = channel_sums.shape
    width = channels // GROUPS
    grouped = channel_sums.reshape(tiles, GROUPS, width).sum(axis=-1) / per_group
    return jnp.repeat(grouped, width, axis=1)


def shifted(padded, tap, tile_side):
    row_off = tap // 3
    col_off = tap % 3
    return lax.dynamic_slice(
        padded,
        (0, row_off, col_off, 0),
        (padded.shape[0], tile_side, tile_side, padded.shape[3]),
    )


def halving_doubling_sum(block, axis):
    size = lax.axis_size(axis)
    levels = size.bit_length() - 1
    if size != 1 << levels or levels == 0:
        return lax.psum(block, axis)
    order = [0, levels - 1] + list(range(1, levels - 1)) if levels > 1 else [0]
    rows = block.shape[0]
    padded_rows = -(-rows // size) * size
    cur = jnp.pad(block, ((0, padded_rows - rows), (0, 0)))
    index = lax.axis_index(axis)
    for level in order:
        half = cur.shape[0] // 2
        low = ((index >> level) & 1) == 0
        send = jnp.where(low, cur[half:], cur[:half])
        keep = jnp.where(low, cur[:half], cur[half:])
        pairs = [(i, i ^ (1 << level)) for i in range(size)]
        cur = keep + lax.ppermute(send, axis, pairs)
    for level in reversed(order):
        low = ((index >> level) & 1) == 0
        pairs = [(i, i ^ (1 << level)) for i in range(size)]
        other = lax.ppermute(cur, axis, pairs)
        cur = jnp.where(low, jnp.concatenate([cur, other]), jnp.concatenate([other, cur]))
    return cur[:rows]


def doubling_sum(block, axis):
    size = lax.axis_size(axis)
    levels = size.bit_length() - 1
    if size != 1 << levels:
        return lax.psum(block, axis)
    for level in range(levels):
        pairs = [(i, i ^ (1 << level)) for i in range(size)]
        block = block + lax.ppermute(block, axis, pairs)
    return block


def exchange_sum(block, axis):
    size = lax.axis_size(axis)
    rows = block.shape[0]
    padded_rows = -(-rows // size) * size
    parts = jnp.pad(block, ((0, padded_rows - rows), (0, 0))).reshape(size, padded_rows // size, -1)
    mine = lax.all_to_all(parts, axis, 0, 0, tiled=False).sum(axis=0)
    spread = jnp.broadcast_to(mine[None], (size,) + mine.shape)
    full = lax.all_to_all(spread, axis, 0, 0, tiled=False)
    return full.reshape(padded_rows, -1)[:rows]


def gathered_sum(block, axis):
    size = lax.axis_size(axis)
    spread = jnp.broadcast_to(block[None], (size,) + block.shape)
    return lax.all_to_all(spread, axis, 0, 0, tiled=False).sum(axis=0)


def body(
    latents,
    bucket,
    cotangent,
    tile_count,
    cond_table,
    norm_gain,
    norm_shift,
    conv_bias,
    down_bias,
    conv_weight,
    down_weight,
):
    slot_total, tile_side, _, channels = latents.shape
    row_block = conv_weight.shape[0]

    live = jnp.arange(slot_total, dtype=jnp.int32) < tile_count[0]
    live4 = live[:, None, None, None]
    masked_cot = jnp.where(live4, cotangent, jnp.zeros_like(cotangent))

    per_group = tile_side * tile_side * (channels // GROUPS)
    values = latents.astype(jnp.float32)
    center = group_mean(jnp.sum(values, axis=(1, 2)), per_group)
    deviation = values - center[:, None, None, :]
    spread = group_mean(jnp.sum(deviation * deviation, axis=(1, 2)), per_group)
    inv_std = lax.rsqrt(spread + 1e-05)[:, None, None, :]
    normed = deviation * inv_std
    pre_act = normed * norm_gain + norm_shift
    sigmoid_v = jax.nn.sigmoid(pre_act)
    activated = (pre_act * sigmoid_v).astype(jnp.bfloat16)
    cot_rows = masked_cot.reshape(-1, channels)
    act_rows = activated.reshape(-1, channels)
    first_parts = (down_weight, cot_rows, act_rows)
    got = lax.all_gather(jnp.concatenate(first_parts, axis=0), "fsdp", axis=0, tiled=False)
    edges = [0]
    for part in first_parts:
        edges.append(edges[-1] + part.shape[0])
    pieces = [got[:, edges[i] : edges[i + 1]] for i in range(len(first_parts))]
    down_kernel = pieces[0].reshape(3, 3, channels, channels)
    cot_all = pieces[1].reshape((-1,) + masked_cot.shape[1:])
    act_all = pieces[2].reshape((-1,) + activated.shape[1:])
    conv_shard, _ = lax.optimization_barrier((conv_weight, got))
    conv_kernel = lax.all_gather(conv_shard, "fsdp", axis=0, tiled=True).reshape(
        3, 3, channels, channels
    )

    conditioning = cond_table[bucket]
    conv_out = lax.conv_general_dilated(
        activated,
        conv_kernel,
        (1, 1),
        ((1, 1), (1, 1)),
        dimension_numbers=CONV_DIMS,
        preferred_element_type=jnp.float32,
    )
    conv_out = conv_out + conv_bias + conditioning[:, None, None, :]
    residual = (values + conv_out).astype(jnp.bfloat16)
    down_out = lax.conv_general_dilated(
        residual,
        down_kernel,
        (2, 2),
        ((1, 1), (1, 1)),
        dimension_numbers=CONV_DIMS,
        preferred_element_type=jnp.float32,
    )
    block_output = (down_out + down_bias).astype(jnp.bfloat16)
    block_output = jnp.where(live4, block_output, jnp.zeros_like(block_output))

    resid_all = lax.conv_general_dilated(
        cot_all,
        down_kernel[::-1, ::-1],
        (1, 1),
        ((1, 2), (1, 2)),
        lhs_dilation=(2, 2),
        dimension_numbers=BACK_DIMS,
        preferred_element_type=jnp.float32,
    )
    hid_all = resid_all.astype(jnp.bfloat16).reshape(-1, channels)
    grad_resid = lax.dynamic_slice_in_dim(
        resid_all, lax.axis_index("fsdp") * slot_total, slot_total, axis=0
    )
    grad_hidden = grad_resid.astype(jnp.bfloat16)
    grad_act = lax.conv_general_dilated(
        grad_hidden,
        conv_kernel[::-1, ::-1],
        (1, 1),
        ((1, 1), (1, 1)),
        dimension_numbers=BACK_DIMS,
        preferred_element_type=jnp.float32,
    )
    grad_pre = grad_act * sigmoid_v * (1.0 + pre_act * (1.0 - sigmoid_v))
    scaled = grad_pre * norm_gain
    mean_one = group_mean(jnp.sum(scaled, axis=(1, 2)), per_group)[:, None, None, :]
    mean_two = group_mean(jnp.sum(scaled * normed, axis=(1, 2)), per_group)[:, None, None, :]
    grad_input = (grad_resid + inv_std * (scaled - mean_one - normed * mean_two)).astype(
        jnp.bfloat16
    )
    affine = jnp.stack(
        [
            jnp.sum(grad_pre * normed, axis=(0, 1, 2)),
            jnp.sum(grad_pre, axis=(0, 1, 2)),
            jnp.sum(grad_resid, axis=(0, 1, 2)),
        ]
    )

    first_row = lax.axis_index("fsdp") * row_block
    first_tap = first_row // channels
    first_chan = first_row % channels
    span = (row_block + channels - 1) // channels + 1
    act_pad = jnp.pad(act_all, ((0, 0), (1, 1), (1, 1), (0, 0)))
    taps = [
        shifted(act_pad, jnp.minimum(first_tap + extra, 8), tile_side) for extra in range(span)
    ]
    tap_cols = jnp.concatenate(taps, axis=-1)
    own_cols = lax.dynamic_slice_in_dim(tap_cols, first_chan, row_block, axis=3)
    weight_term = lax.dot_general(
        own_cols.reshape(-1, row_block),
        hid_all,
        (((0,), (0,)), ((), ())),
        preferred_element_type=jnp.float32,
    )
    loss_scale = 4.0 / math.sqrt(
        tile_side * tile_side * slot_total * lax.axis_size("dp") * lax.axis_size("fsdp")
    )
    grad_conv = exchange_sum(weight_term * loss_scale, "dp")
    grad_affine = gathered_sum(gathered_sum(affine * loss_scale, "fsdp"), "dp")
    return (block_output, grad_input, grad_conv, grad_affine)


def solution(mesh):
    placed = (
        P(("dp", "fsdp"), None, None, None),
        P(("dp", "fsdp")),
        P(("dp", "fsdp"), None, None, None),
        P(("dp", "fsdp")),
        P(),
        P(),
        P(),
        P(),
        P(),
        P("fsdp", None),
        P("fsdp", None),
    )
    return jax.shard_map(
        body,
        mesh=mesh,
        in_specs=placed,
        out_specs=(
            P(("dp", "fsdp"), None, None, None),
            P(("dp", "fsdp"), None, None, None),
            P("fsdp", None),
            P(),
        ),
        check_vma=False,
    )
```

profile of v0, /device:TPU:2, one launch (start us, length us, event | category | flops | bytes accessed | tf_op | source)
XLA Modules:
  0.0 276.8 jit_solution(16127755472243397360)
XLA Ops:
  7.9 1.2 convert_reduce_fusion
  9.1 0.1 reshape.95
  9.3 0.1 reduce_sum.127
  9.4 0.1 sub.36
  9.6 1.3 fusion.35
  10.8 0.1 reshape.96
  11.0 0.1 reduce_sum.129
  11.1 0.1 broadcast_in_dim.29
  11.1 0.1 rsqrt.12
  11.3 1.0 copy_select_fusion
  12.3 1.6 multiply_convert_fusion
  13.9 2.0 pad_maximum_fusion
  16.0 103.4 %all-gather.6.cloned.1.call-done = bf16[10880,640]{1,0:T(8,128)(2,1)} async-done(((bf16[680,640]{1,0:T(8,128)(2,1)}), bf16[10880,640]{1,0:T(8,128)(2,1)}) %all-gather.6.cloned.1.call-update) | async-done | bytes 13926416 | tf_op jit(solution)/shard_map/all_gather | solution.py:116
  119.6 1.4 slice.19
  121.0 5.4 %slice.20 = bf16[16,256,640]{2,1,0:T(8,128)(2,1)} slice(bf16[16,680,640]{2,1,0:T(8,128)(2,1)} %bitcast.26), slice={[0:16], [424:680], [0:640]} | slice | bytes 10485760 | tf_op jit(solution)/shard_map/slice | solution.py:120
  126.5 6.7 %slice.18 = bf16[16,360,640]{2,1,0:T(8,128)(2,1)} slice(bf16[16,680,640]{2,1,0:T(8,128)(2,1)} %bitcast.27), slice={[0:16], [0:360], [0:640]} | slice | bytes 14745600 | tf_op jit(solution)/shard_map/slice | solution.py:120
  133.2 0.3 reshape.101
  133.5 8.0 %copy.40 = bf16[64,8,8,640]{3,0,2,1:T(8,128)(2,1)} copy(bf16[64,8,8,640]{3,2,1,0:T(8,128)(2,1)} %bitcast.24) | data formatting | bytes 10485760 | tf_op jit(solution)/shard_map/reshape | solution.py:123
  141.6 9.6 %pad_dynamic-slice_fusion.2 = (bf16[64,8,8,640]{3,0,2,1:T(8,128)(2,1)}, bf16[64,8,8,640]{3,0,2,1:T(8,128)(2,1)}) fusion(s32[]{:T(128)S(6)} %select_n.63, s32[]{:T(128)S(6)} %select_n.65, bf16[64,8,8,640]{3,0,2,1:T(8,128)(2,1)} %copy.40, s32[]{:T(128)S(6)} %select_n.59, s32[]{:T(128)S(6)} %select_n.61), kind=kLoop, calls=%fused_computation.3 | loop fusion | bytes 15728656 | tf_op jit(solution)/shard_map/dynamic_slice | solution.py:23
  151.2 16.6 %fusion.14 = f32[64,8,8,640]{3,0,2,1:T(8,128)S(1)} fusion(bf16[3,3,640,640]{3,2,1,0:T(8,128)(2,1)} %bitcast.22, bf16[64,4,4,640]{3,2,1,0:T(4,128)(2,1)S(1)} %reshape.101), kind=kOutput, calls=%fused_computation.10 | convolution fusion | flops 6343884800 | bytes 19169280 | tf_op jit(solution)/shard_map/conv_general_dilated | solution.py:151
  167.8 4.6 %fusion.9 = f32[360,640]{1,0:T(8,128)S(1)} fusion(f32[64,8,8,640]{3,0,2,1:T(8,128)S(1)} %fusion.14, s32[]{:T(128)S(6)} %select_n.67, bf16[64,8,8,640]{3,0,2,1:T(8,128)(2,1)S(1)} %copy-done.3, bf16[64,8,8,640]{3,0,2,1:T(8,128)(2,1)S(1)} %copy-done.2), kind=kOutput, calls=%fused_computation.9 | convolution fusion | flops 1896186880 | bytes 21893124 | tf_op jit(solution)/shard_map/dot_general | solution.py:198
  172.5 1.1 reshape.105
  173.7 7.1 %all-to-all-start = ((f32[16,23,640]{2,1,0:T(8,128)}), f32[16,23,640]{2,1,0:T(8,128)S(1)}, u32[]{:S(2)}, u32[]{:S(2)}) async-start(f32[16,23,640]{2,1,0:T(8,128)} %reshape.105), calls=%async_computation | async-start | bytes 1966080 | tf_op jit(solution)/shard_map/all_to_all | solution.py:71
  180.8 26.2 %all-to-all-done = f32[16,23,640]{2,1,0:T(8,128)S(1)} async-done(((f32[16,23,640]{2,1,0:T(8,128)}), f32[16,23,640]{2,1,0:T(8,128)S(1)}, u32[]{:S(2)}, u32[]{:S(2)}) %all-to-all-start) | async-done | bytes 942112 | tf_op jit(solution)/shard_map/all_to_all | solution.py:71
  207.1 1.1 broadcast_in_dim.58
  208.1 4.3 %all-to-all-start.1 = ((f32[16,23,640]{2,1,0:T(8,128)}), f32[16,23,640]{2,1,0:T(8,128)S(1)}, u32[]{:S(2)}, u32[]{:S(2)}) async-start(f32[16,23,640]{2,1,0:T(8,128)} %broadcast_in_dim.58), calls=%async_computation.1 | async-start | bytes 1966080 | tf_op jit(solution)/shard_map/all_to_all | solution.py:73
  212.5 8.1 %fusion.34 = (f32[640]{0:T(1024)S(1)}, f32[4,640]{1,0:T(4,128)S(1)}, f32[4,640]{1,0:T(4,128)S(1)}, f32[640]{0:T(1024)S(1)}, f32[4,8,8,640]{3,0,2,1:T(4,128)S(1)}) fusion(f32[4,640]{1,0:T(4,128)S(1)} %rsqrt.12, f32[4,640]{1,0:T(4,128)S(1)} %sub.36, bf16[4,8,8,640]{3,2,1,0:T(8,128)(2,1)S(1)} %copy-done.4, f32[640]{0:T(1024)S(1)} %copy-done.5, ...), kind=kOutput, calls=%fused_computation.36 | convolution fusion | flops 1589241600 | bytes 8734724 | tf_op jit(solution)/shard_map/conv_general_dilated | solution.py:165
  220.7 0.1 reshape.103
  220.8 0.1 reduce_sum.133
  220.9 0.1 broadcast_in_dim.57
  221.0 0.1 mul.93
  221.1 0.1 reshape.102
  221.2 0.1 reduce_sum.131
  221.4 0.1 sub.40
  221.5 2.0 dynamic-slice_reduce_fusion
  223.6 14.8 %all-to-all-done.1 = f32[16,23,640]{2,1,0:T(8,128)S(1)} async-done(((f32[16,23,640]{2,1,0:T(8,128)}), f32[16,23,640]{2,1,0:T(8,128)S(1)}, u32[]{:S(2)}, u32[]{:S(2)}) %all-to-all-start.1) | async-done | bytes 942112 | tf_op jit(solution)/shard_map/all_to_all | solution.py:73
  238.4 0.7 broadcast_in_dim.59
  239.1 5.9 %all-to-all-start.2 = ((f32[16,3,640]{2,1,0:T(4,128)}), f32[16,3,640]{2,1,0:T(4,128)S(1)}, u32[]{:S(2)}, u32[]{:S(2)}) async-start(f32[16,3,640]{2,1,0:T(4,128)} %broadcast_in_dim.59), calls=%async_computation.2 | async-start | bytes 327680 | tf_op jit(solution)/shard_map/all_to_all | solution.py:80
  245.0 0.6 gather_fusion
  245.6 0.1 reshape.106
  245.7 1.0 slice.21
  246.7 4.7 %all-to-all-done.2 = f32[16,3,640]{2,1,0:T(4,128)S(1)} async-done(((f32[16,3,640]{2,1,0:T(4,128)}), f32[16,3,640]{2,1,0:T(4,128)S(1)}, u32[]{:S(2)}, u32[]{:S(2)}) %all-to-all-start.2) | async-done | bytes 122912 | tf_op jit(solution)/shard_map/all_to_all | solution.py:80
  251.5 0.7 broadcast_in_dim.60
  252.2 3.8 %all-to-all-start.3 = ((f32[16,3,640]{2,1,0:T(4,128)}), f32[16,3,640]{2,1,0:T(4,128)S(1)}, u32[]{:S(2)}, u32[]{:S(2)}) async-start(f32[16,3,640]{2,1,0:T(4,128)} %broadcast_in_dim.60), calls=%async_computation.3 | async-start | bytes 327680 | tf_op jit(solution)/shard_map/all_to_all | solution.py:80
  256.0 11.9 %fusion.21 = bf16[4,4,4,640]{3,0,2,1:T(4,128)(2,1)S(1)} fusion(bf16[3,3,640,640]{3,2,1,0:T(8,128)(2,1)} %bitcast.23, f32[640]{0:T(1024)S(1)} %copy-done.7, pred[4]{0:T(512)(128)(4,1)S(1)} %iota_compare_fusion, bf16[3,3,640,640]{3,2,1,0:T(8,128)(2,1)} %bitcast.30, f32[4,640]{1,0:T(4,128)S(1)} %gather_fusion, f32[640]{0:T(1024)S(1)} %copy-done.8, ...), kind=kOutput, calls=%fused_computation.20 | convolution fusion | flops 1985044480 | bytes 15196164 | tf_op jit(solution)/shard_map/conv_general_dilated | solution.py:140
  267.9 0.7 copy.43
  268.5 0.8 copy.44
  269.3 0.6 reduce_sum.139
  (45 shorter events, 0.7 us)
Async XLA Ops:
  7.2 237.9 %copy-start = (f32[40,640]{1,0:T(8,128)S(1)}, f32[40,640]{1,0:T(8,128)}, u32[]{:S(2)}) copy-start(f32[40,640]{1,0:T(8,128)} %param.15) | copy-start | bytes 307204
  7.2 112.3 %all-gather.6.cloned.1.call-start = ((), (), s32[]{:S(2)}) async-start(), calls=%async_computation.5 | async-start | bytes 14796800 | tf_op jit(solution)/shard_map/all_gather | solution.py:116
  16.0 196.5 %all-gather.4.cloned.1.call-start = ((), (), s32[]{:S(2)}) async-start(), calls=%async_computation.4 | async-start | bytes 7833600 | tf_op jit(solution)/shard_map/all_gather | solution.py:125
  151.2 16.6 %copy-start.2 = (bf16[64,8,8,640]{3,0,2,1:T(8,128)(2,1)S(1)}, bf16[64,8,8,640]{3,0,2,1:T(8,128)(2,1)}, u32[]{:S(2)}) copy-start(bf16[64,8,8,640]{3,0,2,1:T(8,128)(2,1)} %get-tuple-element.28) | copy-start | bytes 15728644
  151.2 16.6 %copy-start.3 = (bf16[64,8,8,640]{3,0,2,1:T(8,128)(2,1)S(1)}, bf16[64,8,8,640]{3,0,2,1:T(8,128)(2,1)}, u32[]{:S(2)}) copy-start(bf16[64,8,8,640]{3,0,2,1:T(8,128)(2,1)} %get-tuple-element.29) | copy-start | bytes 15728644
  167.8 4.6 %copy-start.1 = (f32[64,8,8,640]{3,0,2,1:T(8,128)}, f32[64,8,8,640]{3,0,2,1:T(8,128)S(1)}, u32[]{:S(2)}) copy-start(f32[64,8,8,640]{3,0,2,1:T(8,128)S(1)} %fusion.14) | copy-start | bytes 31457284
  172.4 40.1 %copy-start.4 = (bf16[4,8,8,640]{3,2,1,0:T(8,128)(2,1)S(1)}, bf16[4,8,8,640]{3,2,1,0:T(8,128)(2,1)}, u32[]{:S(2)}) copy-start(bf16[4,8,8,640]{3,2,1,0:T(8,128)(2,1)} %param.11) | copy-start | bytes 983044
  172.4 40.1 %copy-start.5 = (f32[640]{0:T(1024)S(1)}, f32[640]{0:T(1024)}, u32[]{:S(2)}) copy-start(f32[640]{0:T(1024)} %param.16) | copy-start | bytes 7684
  172.4 40.1 %copy-start.6 = (f32[640]{0:T(1024)S(1)}, f32[640]{0:T(1024)}, u32[]{:S(2)}) copy-start(f32[640]{0:T(1024)} %param.17) | copy-start | bytes 7684
  173.7 33.3 %all-to-all-start = ((f32[16,23,640]{2,1,0:T(8,128)}), f32[16,23,640]{2,1,0:T(8,128)S(1)}, u32[]{:S(2)}, u32[]{:S(2)}) async-start(f32[16,23,640]{2,1,0:T(8,128)} %reshape.105), calls=%async_computation | async-start | bytes 1966080 | tf_op jit(solution)/shard_map/all_to_all | solution.py:71
  208.1 30.3 %all-to-all-start.1 = ((f32[16,23,640]{2,1,0:T(8,128)}), f32[16,23,640]{2,1,0:T(8,128)S(1)}, u32[]{:S(2)}, u32[]{:S(2)}) async-start(f32[16,23,640]{2,1,0:T(8,128)} %broadcast_in_dim.58), calls=%async_computation.1 | async-start | bytes 1966080 | tf_op jit(solution)/shard_map/all_to_all | solution.py:73
  212.5 32.5 %copy-start.9 = (s32[4]{0:T(128)S(1)}, s32[4]{0:T(128)}, u32[]{:S(2)}) copy-start(s32[4]{0:T(128)} %param.12) | copy-start | bytes 52
  220.6 35.3 %copy-start.7 = (f32[640]{0:T(1024)S(1)}, f32[640]{0:T(1024)}, u32[]{:S(2)}) copy-start(f32[640]{0:T(1024)} %param.19) | copy-start | bytes 7684
  220.6 35.3 %copy-start.8 = (f32[640]{0:T(1024)S(1)}, f32[640]{0:T(1024)}, u32[]{:S(2)}) copy-start(f32[640]{0:T(1024)} %param.18) | copy-start | bytes 7684
  239.1 12.3 %all-to-all-start.2 = ((f32[16,3,640]{2,1,0:T(4,128)}), f32[16,3,640]{2,1,0:T(4,128)S(1)}, u32[]{:S(2)}, u32[]{:S(2)}) async-start(f32[16,3,640]{2,1,0:T(4,128)} %broadcast_in_dim.59), calls=%async_computation.2 | async-start | bytes 327680 | tf_op jit(solution)/shard_map/all_to_all | solution.py:80
  252.2 17.1 %all-to-all-start.3 = ((f32[16,3,640]{2,1,0:T(4,128)}), f32[16,3,640]{2,1,0:T(4,128)S(1)}, u32[]{:S(2)}, u32[]{:S(2)}) async-start(f32[16,3,640]{2,1,0:T(4,128)} %broadcast_in_dim.60), calls=%async_computation.3 | async-start | bytes 327680 | tf_op jit(solution)/shard_map/all_to_all | solution.py:80
Sparse Core Ops, SparseCore 0:
  16.1 103.3 all-gather.5
  122.2 72.2 all-gather.3
where the time goes:
time: 280 us; the launch traced here: 277 us
  waiting for transfers between devices  149 us (53%)
  matrix products  41.1 us (15%)
  local copies, waits for them, and re-layouts  39.8 us (14%)
  starting transfers between devices  21.2 us (8%)
  between operations  15.2 us (5%)
  other arithmetic  10.2 us (4%)
    all_gather x1, waiting for transfers between devices, body(): lax.all_gather(jnp.concatenate(first_parts, axis=0), 'fsdp', axis=0, tile...  103 us
    all_to_all x1, waiting for transfers between devices, exchange_sum(): mine = lax.all_to_all(parts, axis, 0, 0, tiled=False).sum(axis=0)  26.2 us
    conv_general_dilated x1, matrix products, body(): lax.conv_general_dilated(cot_all, down_kernel[::-1, ::-1], (1, 1), ((1, 2...  16.6 us
    all_to_all x1, waiting for transfers between devices, exchange_sum(): full = lax.all_to_all(spread, axis, 0, 0, tiled=False)  14.8 us
    slice x3, local copies, waits for them, and re-layouts, body(): pieces = [got[:, edges[i]:edges[i + 1]] for i in range(len(first_parts))]  13.6 us
    conv_general_dilated x1, matrix products, body(): lax.conv_general_dilated(residual, down_kernel, (2, 2), ((1, 1), (1, 1)),...  11.9 us
    all_to_all x2, starting transfers between devices, gathered_sum(): return lax.all_to_all(spread, axis, 0, 0, tiled=False).sum(axis=0)  9.67 us
    dynamic_slice x1, local copies, waits for them, and re-layouts, shifted(): lax.dynamic_slice(padded, (0, row_off, col_off, 0), (padded.shape[0], til...  9.64 us
  transfers between devices with their start and end apart: 6, of which 4 were waited for; matrix products, arithmetic and copies ran while one was open for 29% of the time, Pallas kernels for 0%

commit v1 on v0

--- a/solution.py
+++ b/solution.py
@@ -78,6 +78,20 @@
     size = lax.axis_size(axis)
     spread = jnp.broadcast_to(block[None], (size,) + block.shape)
     return lax.all_to_all(spread, axis, 0, 0, tiled=False).sum(axis=0)
+
+
+def exchange_sum_with(block, extra, axis):
+    size = lax.axis_size(axis)
+    rows = block.shape[0]
+    padded_rows = -(-rows // size) * size
+    chunk = padded_rows // size
+    parts = jnp.pad(block, ((0, padded_rows - rows), (0, 0))).reshape(size, chunk, -1)
+    mine = lax.all_to_all(parts, axis, 0, 0, tiled=False).sum(axis=0)
+    payload = jnp.concatenate([mine, extra], axis=0)
+    spread = jnp.broadcast_to(payload[None], (size,) + payload.shape)
+    full = lax.all_to_all(spread, axis, 0, 0, tiled=False)
+    summed = full[:, :chunk].reshape(padded_rows, -1)[:rows]
+    return summed, full[:, chunk:].sum(axis=0)
 
 
 def body(
@@ -204,8 +218,8 @@
     loss_scale = 4.0 / math.sqrt(
         tile_side * tile_side * slot_total * lax.axis_size("dp") * lax.axis_size("fsdp")
     )
-    grad_conv = exchange_sum(weight_term * loss_scale, "dp")
-    grad_affine = gathered_sum(gathered_sum(affine * loss_scale, "fsdp"), "dp")
+    affine_fsdp = gathered_sum(affine * loss_scale, "fsdp")
+    grad_conv, grad_affine = exchange_sum_with(weight_term * loss_scale, affine_fsdp, "dp")
     return (block_output, grad_input, grad_conv, grad_affine)
 
 

time: 280 us -> 272 us (0.971)
  waiting for transfers between devices: 149 us -> 144 us
    all_to_all x2, waiting for transfers between devices: 41 us -> 20.9 us  [the longest x1 19.5 us: exchange_sum_with(): full = lax.all_to_all(spread, axis, 0, 0, tiled=False)]
    all_gather x1, waiting for transfers between devices: 0.02 us -> 13.7 us  [body(): lax.all_gather(conv_shard, 'fsdp', axis=0, tiled=True)]
    all_to_all x2 -> x1, starting transfers between devices: 9.67 us -> 5.88 us  [gathered_sum(): return lax.all_to_all(spread, axis, 0, 0, tiled=False).sum(axis=0)]
    all_to_all x2 -> x1, waiting for transfers between devices: 4.72 us -> 6.38 us  [gathered_sum(): return lax.all_to_all(spread, axis, 0, 0, tiled=False).sum(axis=0)]
  transfers between devices with their start and end apart: 6 -> 5, of which waited for: 4 -> 5; matrix products, arithmetic and copies ran while one was open for 29% -> 29% of each run, Pallas kernels for 0% -> 0%
where the time goes in v1:
time: 272 us; the launch traced here: 271 us
  waiting for transfers between devices  144 us (53%)
  local copies, waits for them, and re-layouts  41.4 us (15%)
  matrix products  41.1 us (15%)
  starting transfers between devices  19.1 us (7%)
  between operations  15.2 us (6%)
  other arithmetic  10.2 us (4%)
    all_gather x1, waiting for transfers between devices, body(): lax.all_gather(jnp.concatenate(first_parts, axis=0), 'fsdp', axis=0, tile...  103 us
    all_to_all x1, waiting for transfers between devices, exchange_sum_with(): full = lax.all_to_all(spread, axis, 0, 0, tiled=False)  19.5 us
    conv_general_dilated x1, matrix products, body(): lax.conv_general_dilated(cot_all, down_kernel[::-1, ::-1], (1, 1), ((1, 2...  16.6 us
    all_gather x1, waiting for transfers between devices, body(): lax.all_gather(conv_shard, 'fsdp', axis=0, tiled=True)  13.7 us
    slice x3, local copies, waits for them, and re-layouts, body(): pieces = [got[:, edges[i]:edges[i + 1]] for i in range(len(first_parts))]  13.6 us
    conv_general_dilated x1, matrix products, body(): lax.conv_general_dilated(residual, down_kernel, (2, 2), ((1, 1), (1, 1)),...  11.9 us
    dynamic_slice x1, local copies, waits for them, and re-layouts, shifted(): lax.dynamic_slice(padded, (0, row_off, col_off, 0), (padded.shape[0], til...  9.64 us
    conv_general_dilated x1, matrix products, body(): lax.conv_general_dilated(grad_hidden, conv_kernel[::-1, ::-1], (1, 1), ((...  8.06 us
  transfers between devices with their start and end apart: 5, of which 5 were waited for; matrix products, arithmetic and copies ran while one was open for 29% of the time, Pallas kernels for 0%

profile of v1, /device:TPU:2, one launch (start us, length us, event | category | flops | bytes accessed | tf_op | source)
XLA Modules:
  0.0 271.5 jit_solution(7952355148541512620)
XLA Ops:
  7.9 1.2 convert_reduce_fusion
  9.1 0.1 reshape.94
  9.3 0.1 reduce_sum.127
  9.4 0.1 broadcast_in_dim.26
  9.4 0.1 sub.36
  9.6 1.3 fusion.35
  10.8 0.1 reshape.95
  11.0 0.1 reduce_sum.129
  11.1 0.1 broadcast_in_dim.48
  11.1 0.1 rsqrt.12
  11.3 1.0 copy_select_fusion
  12.3 1.6 multiply_convert_fusion
  13.9 2.0 pad_maximum_fusion
  16.0 103.4 %all-gather.6.cloned.1.call-done = bf16[10880,640]{1,0:T(8,128)(2,1)} async-done(((bf16[680,640]{1,0:T(8,128)(2,1)}), bf16[10880,640]{1,0:T(8,128)(2,1)}) %all-gather.6.cloned.1.call-update) | async-done | bytes 13926416 | tf_op jit(solution)/shard_map/all_gather | solution.py:130
  119.6 1.4 slice.27
  121.0 5.4 %slice.28 = bf16[16,256,640]{2,1,0:T(8,128)(2,1)} slice(bf16[16,680,640]{2,1,0:T(8,128)(2,1)} %bitcast.26), slice={[0:16], [424:680], [0:640]} | slice | bytes 10485760 | tf_op jit(solution)/shard_map/slice | solution.py:134
  126.5 6.7 %slice.26 = bf16[16,360,640]{2,1,0:T(8,128)(2,1)} slice(bf16[16,680,640]{2,1,0:T(8,128)(2,1)} %bitcast.27), slice={[0:16], [0:360], [0:640]} | slice | bytes 14745600 | tf_op jit(solution)/shard_map/slice | solution.py:134
  133.2 0.3 reshape.100
  133.5 8.0 %copy.40 = bf16[64,8,8,640]{3,0,2,1:T(8,128)(2,1)} copy(bf16[64,8,8,640]{3,2,1,0:T(8,128)(2,1)} %bitcast.24) | data formatting | bytes 10485760 | tf_op jit(solution)/shard_map/reshape | solution.py:137
  141.6 9.6 %pad_dynamic-slice_fusion.2 = (bf16[64,8,8,640]{3,0,2,1:T(8,128)(2,1)}, bf16[64,8,8,640]{3,0,2,1:T(8,128)(2,1)}) fusion(s32[]{:T(128)S(6)} %select_n.63, s32[]{:T(128)S(6)} %select_n.65, bf16[64,8,8,640]{3,0,2,1:T(8,128)(2,1)} %copy.40, s32[]{:T(128)S(6)} %select_n.59, s32[]{:T(128)S(6)} %select_n.61), kind=kLoop, calls=%fused_computation.3 | loop fusion | bytes 15728656 | tf_op jit(solution)/shard_map/dynamic_slice | solution.py:23
  151.2 16.6 %fusion.14 = f32[64,8,8,640]{3,0,2,1:T(8,128)S(1)} fusion(bf16[3,3,640,640]{3,2,1,0:T(8,128)(2,1)} %bitcast.22, bf16[64,4,4,640]{3,2,1,0:T(4,128)(2,1)S(1)} %reshape.100), kind=kOutput, calls=%fused_computation.10 | convolution fusion | flops 6343884800 | bytes 19169280 | tf_op jit(solution)/shard_map/conv_general_dilated | solution.py:165
  167.8 4.6 %fusion.9 = f32[360,640]{1,0:T(8,128)S(1)} fusion(f32[64,8,8,640]{3,0,2,1:T(8,128)S(1)} %fusion.14, s32[]{:T(128)S(6)} %select_n.67, bf16[64,8,8,640]{3,0,2,1:T(8,128)(2,1)S(1)} %copy-done.3, bf16[64,8,8,640]{3,0,2,1:T(8,128)(2,1)S(1)} %copy-done.2), kind=kOutput, calls=%fused_computation.9 | convolution fusion | flops 1896186880 | bytes 21893124 | tf_op jit(solution)/shard_map/dot_general | solution.py:212
  172.5 1.1 reshape.104
  173.6 7.2 %all-to-all-start = ((f32[16,23,640]{2,1,0:T(8,128)}), f32[16,23,640]{2,1,0:T(8,128)S(1)}, u32[]{:S(2)}, u32[]{:S(2)}) async-start(f32[16,23,640]{2,1,0:T(8,128)} %reshape.104), calls=%async_computation | async-start | bytes 1966080 | tf_op jit(solution)/shard_map/all_to_all | solution.py:89
  180.8 13.7 %all-gather.4.cloned.1.call-done = bf16[5760,640]{1,0:T(8,128)(2,1)} async-done(((bf16[360,640]{1,0:T(8,128)(2,1)}), bf16[5760,640]{1,0:T(8,128)(2,1)}) %all-gather.4.cloned.1.call-update) | async-done | bytes 7372816 | tf_op jit(solution)/shard_map/all_gather | solution.py:139
  194.5 8.1 %fusion.34 = (f32[640]{0:T(1024)S(1)}, f32[4,640]{1,0:T(4,128)S(1)}, f32[4,640]{1,0:T(4,128)S(1)}, f32[640]{0:T(1024)S(1)}, f32[4,8,8,640]{3,0,2,1:T(4,128)S(1)}) fusion(f32[4,640]{1,0:T(4,128)S(1)} %rsqrt.12, f32[4,640]{1,0:T(4,128)S(1)} %sub.36, bf16[4,8,8,640]{3,2,1,0:T(8,128)(2,1)S(1)} %copy-done.4, f32[640]{0:T(1024)S(1)} %copy-done.5, ...), kind=kOutput, calls=%fused_computation.36 | convolution fusion | flops 1589241600 | bytes 8734724 | tf_op jit(solution)/shard_map/conv_general_dilated | solution.py:179
  202.6 0.1 reshape.102
  202.8 0.1 reduce_sum.133
  202.9 0.1 broadcast_in_dim.51
  202.9 0.1 mul.93
  203.1 0.1 reshape.101
  203.2 0.1 reduce_sum.131
  203.4 0.1 sub.40
  203.5 2.0 dynamic-slice_reduce_fusion
  205.6 1.4 all-to-all-done
  207.0 0.7 broadcast_in_dim.52
  207.7 5.9 %all-to-all-start.1 = ((f32[16,3,640]{2,1,0:T(4,128)}), f32[16,3,640]{2,1,0:T(4,128)S(1)}, u32[]{:S(2)}, u32[]{:S(2)}) async-start(f32[16,3,640]{2,1,0:T(4,128)} %broadcast_in_dim.52), calls=%async_computation.1 | async-start | bytes 327680 | tf_op jit(solution)/shard_map/all_to_all | solution.py:80
  213.6 6.4 %all-to-all-done.1 = f32[16,3,640]{2,1,0:T(4,128)S(1)} async-done(((f32[16,3,640]{2,1,0:T(4,128)}), f32[16,3,640]{2,1,0:T(4,128)S(1)}, u32[]{:S(2)}, u32[]{:S(2)}) %all-to-all-start.1) | async-done | bytes 122912 | tf_op jit(solution)/shard_map/all_to_all | solution.py:80
  220.1 1.2 broadcast_in_dim.53
  221.3 5.9 %all-to-all-start.2 = ((f32[16,26,640]{2,1,0:T(8,128)}), f32[16,26,640]{2,1,0:T(8,128)S(1)}, u32[]{:S(2)}, u32[]{:S(2)}) async-start(f32[16,26,640]{2,1,0:T(8,128)} %broadcast_in_dim.53), calls=%async_computation.2 | async-start | bytes 2621440 | tf_op jit(solution)/shard_map/all_to_all | solution.py:92
  227.3 0.6 gather_fusion
  227.8 11.9 %fusion.21 = bf16[4,4,4,640]{3,0,2,1:T(4,128)(2,1)S(1)} fusion(bf16[3,3,640,640]{3,2,1,0:T(8,128)(2,1)} %bitcast.23, f32[640]{0:T(1024)S(1)} %copy-done.7, pred[4]{0:T(512)(128)(4,1)S(1)} %iota_compare_fusion, bf16[3,3,640,640]{3,2,1,0:T(8,128)(2,1)} %bitcast.30, f32[4,640]{1,0:T(4,128)S(1)} %gather_fusion, f32[640]{0:T(1024)S(1)} %copy-done.8, ...), kind=kOutput, calls=%fused_computation.20 | convolution fusion | flops 1985044480 | bytes 15196164 | tf_op jit(solution)/shard_map/conv_general_dilated | solution.py:154
  239.7 0.7 copy.42
  240.4 0.8 copy.43
  241.2 19.5 %all-to-all-done.2 = f32[16,26,640]{2,1,0:T(8,128)S(1)} async-done(((f32[16,26,640]{2,1,0:T(8,128)}), f32[16,26,640]{2,1,0:T(8,128)S(1)}, u32[]{:S(2)}, u32[]{:S(2)}) %all-to-all-start.2) | async-done | bytes 1064992 | tf_op jit(solution)/shard_map/all_to_all | solution.py:92
  260.7 1.1 reshape.105
  261.8 2.2 slice.30
  264.0 0.7 slice_reduce_fusion
  (44 shorter events, 0.6 us)
Async XLA Ops:
  7.2 220.1 %copy-start = (f32[40,640]{1,0:T(8,128)S(1)}, f32[40,640]{1,0:T(8,128)}, u32[]{:S(2)}) copy-start(f32[40,640]{1,0:T(8,128)} %param.15) | copy-start | bytes 307204
  7.2 112.3 %all-gather.6.cloned.1.call-start = ((), (), s32[]{:S(2)}) async-start(), calls=%async_computation.4 | async-start | bytes 14796800 | tf_op jit(solution)/shard_map/all_gather | solution.py:130
  16.0 178.5 %all-gather.4.cloned.1.call-start = ((), (), s32[]{:S(2)}) async-start(), calls=%async_computation.3 | async-start | bytes 7833600 | tf_op jit(solution)/shard_map/all_gather | solution.py:139
  151.2 16.6 %copy-start.2 = (bf16[64,8,8,640]{3,0,2,1:T(8,128)(2,1)S(1)}, bf16[64,8,8,640]{3,0,2,1:T(8,128)(2,1)}, u32[]{:S(2)}) copy-start(bf16[64,8,8,640]{3,0,2,1:T(8,128)(2,1)} %get-tuple-element.28) | copy-start | bytes 15728644
  151.2 16.6 %copy-start.3 = (bf16[64,8,8,640]{3,0,2,1:T(8,128)(2,1)S(1)}, bf16[64,8,8,640]{3,0,2,1:T(8,128)(2,1)}, u32[]{:S(2)}) copy-start(bf16[64,8,8,640]{3,0,2,1:T(8,128)(2,1)} %get-tuple-element.29) | copy-start | bytes 15728644
  167.8 4.6 %copy-start.1 = (f32[64,8,8,640]{3,0,2,1:T(8,128)}, f32[64,8,8,640]{3,0,2,1:T(8,128)S(1)}, u32[]{:S(2)}) copy-start(f32[64,8,8,640]{3,0,2,1:T(8,128)S(1)} %fusion.14) | copy-start | bytes 31457284
  172.4 22.1 %copy-start.4 = (bf16[4,8,8,640]{3,2,1,0:T(8,128)(2,1)S(1)}, bf16[4,8,8,640]{3,2,1,0:T(8,128)(2,1)}, u32[]{:S(2)}) copy-start(bf16[4,8,8,640]{3,2,1,0:T(8,128)(2,1)} %param.11) | copy-start | bytes 983044
  172.4 22.1 %copy-start.5 = (f32[640]{0:T(1024)S(1)}, f32[640]{0:T(1024)}, u32[]{:S(2)}) copy-start(f32[640]{0:T(1024)} %param.16) | copy-start | bytes 7684
  172.4 22.1 %copy-start.6 = (f32[640]{0:T(1024)S(1)}, f32[640]{0:T(1024)}, u32[]{:S(2)}) copy-start(f32[640]{0:T(1024)} %param.17) | copy-start | bytes 7684
  173.6 33.4 %all-to-all-start = ((f32[16,23,640]{2,1,0:T(8,128)}), f32[16,23,640]{2,1,0:T(8,128)S(1)}, u32[]{:S(2)}, u32[]{:S(2)}) async-start(f32[16,23,640]{2,1,0:T(8,128)} %reshape.104), calls=%async_computation | async-start | bytes 1966080 | tf_op jit(solution)/shard_map/all_to_all | solution.py:89
  202.6 24.6 %copy-start.9 = (s32[4]{0:T(128)S(1)}, s32[4]{0:T(128)}, u32[]{:S(2)}) copy-start(s32[4]{0:T(128)} %param.12) | copy-start | bytes 52
  202.6 25.2 %copy-start.7 = (f32[640]{0:T(1024)S(1)}, f32[640]{0:T(1024)}, u32[]{:S(2)}) copy-start(f32[640]{0:T(1024)} %param.19) | copy-start | bytes 7684
  202.6 25.2 %copy-start.8 = (f32[640]{0:T(1024)S(1)}, f32[640]{0:T(1024)}, u32[]{:S(2)}) copy-start(f32[640]{0:T(1024)} %param.18) | copy-start | bytes 7684
  207.7 12.3 %all-to-all-start.1 = ((f32[16,3,640]{2,1,0:T(4,128)}), f32[16,3,640]{2,1,0:T(4,128)S(1)}, u32[]{:S(2)}, u32[]{:S(2)}) async-start(f32[16,3,640]{2,1,0:T(4,128)} %broadcast_in_dim.52), calls=%async_computation.1 | async-start | bytes 327680 | tf_op jit(solution)/shard_map/all_to_all | solution.py:80
  221.3 39.4 %all-to-all-start.2 = ((f32[16,26,640]{2,1,0:T(8,128)}), f32[16,26,640]{2,1,0:T(8,128)S(1)}, u32[]{:S(2)}, u32[]{:S(2)}) async-start(f32[16,26,640]{2,1,0:T(8,128)} %broadcast_in_dim.53), calls=%async_computation.2 | async-start | bytes 2621440 | tf_op jit(solution)/shard_map/all_to_all | solution.py:92
Sparse Core Ops, SparseCore 0:
  16.1 103.3 all-gather.5
  122.2 72.2 all-gather.3
